TPU v7x, 512 devices: a whole 4x8x8 slice. The times are simulated.
512 devices in a mesh: dp: 16 (over y, core), ctx: 32 (over z, x).
Axes of the slice: x: 4, y: 8, z: 8, core: 2. Of those that a mesh axis runs over, the one named last changes fastest.
Arguments:
- inner_gate: bfloat16 [65536, 1024], P(('dp', 'ctx')), parts along dimension 0, may hold values from -6 to 6
- outer_gate: bfloat16 [65536, 1024], P(('dp', 'ctx')), parts along dimension 0, may hold values from -6 to 6
- signal: bfloat16 [65536, 1024], P(('dp', 'ctx')), parts along dimension 0, may hold values from -6 to 6
- filters: float32 [64, 128], replicated, may hold values from -0.5 to 0.5
- bypass: float32 [1024], replicated, may hold values from 0.5 to 1.5
- query_rows: bfloat16 [65536, 1024], P(('dp', 'ctx')), parts along dimension 0, may hold values from -25 to 25
- key_rows: bfloat16 [65536, 1024], P(('dp', 'ctx')), parts along dimension 0, may hold values from -4.5 to 4.5
Outputs:
- hyena_out: bfloat16 [65536, 1024], P(('dp', 'ctx')), parts along dimension 0
- attended: bfloat16 [65536, 1024], P(('dp', 'ctx')), parts along dimension 0
There are 16 independent parts, one for each index of `dp`. A program takes and returns all parts, laid end to end along the dimension named above; an argument that names none is the same for every part. Nothing has to cross between parts.
All inputs are finite; a program needn't handle non-finite values.
Results may differ from a plain program's by a relative error of at most 0.006.
Values may be sent and summed in bfloat16 or wider, within the bound.
No kernel may reach another device: no remote copies, remote signals or barrier semaphores. Data moves between devices by JAX's collectives and lax.ppermute only.
A program may use at most 128 MiB of HBM per device.

v0:
```python
import math
import jax
import jax.numpy as jnp
from jax import lax
from jax.sharding import PartitionSpec as P

DH = 128
TAPS = 128


def passed_along(array, axis, by):
    devices = lax.axis_size(axis)
    return lax.ppermute(array, axis, [(i, (i + by) % devices) for i in range(devices)])


def passed_along_2(array, axis, by):
    devices = lax.axis_size(axis)
    pairs = [(i, i + by) for i in range(devices) if 0 <= i + by < devices]
    return lax.ppermute(array, axis, pairs)


def attend(queries, query_pos, key_rows, hyena_out):
    local_rows, channels = queries.shape
    head_count = channels // DH
    query_heads = queries.reshape(local_rows, head_count, DH)
    latest = jnp.max(query_pos)
    inv_root = 1.0 / math.sqrt(DH)

    def update_block(current, key_piece, value_piece, start):
        running_max, running_sum, weighted = current
        piece_rows = key_piece.shape[0]
        key_pos = start + jnp.arange(piece_rows, dtype=jnp.int32)
        key_heads = key_piece.reshape(piece_rows, head_count, DH)
        value_heads = value_piece.reshape(piece_rows, head_count, DH)
        scores = (
            jnp.einsum("thd,phd->thp", query_heads, key_heads, preferred_element_type=jnp.float32)
            * inv_root
        )
        visible = key_pos[None, None, :] <= query_pos[:, None, None]
        scores = jnp.where(visible, scores, -1e30)
        new_max = jnp.maximum(running_max, jnp.max(scores, axis=2))
        weights = jnp.where(visible, jnp.exp(scores - new_max[:, :, None]), 0.0)
        rescale = jnp.exp(running_max - new_max)
        running_sum = running_sum * rescale + jnp.sum(weights, axis=2)
        weighted = weighted * rescale[:, :, None] + jnp.einsum(
            "thp,phd->thd",
            weights.astype(jnp.bfloat16),
            value_heads,
            preferred_element_type=jnp.float32,
        )
        return (new_max, running_sum, weighted)

    def guarded(current, key_piece, value_piece, start):

        def unchanged(state):
            return state

        def changed(state):
            return update_block(state, key_piece, value_piece, start)

        return lax.cond(start > latest, unchanged, changed, current)

    def fold(softmax_state, pieces, start):
        key_piece, value_piece = pieces
        piece_rows = key_piece.shape[0]
        return guarded(softmax_state, key_piece, value_piece, start)

    initial = (
        jnp.full((local_rows, head_count), -1e30, jnp.float32),
        jnp.zeros((local_rows, head_count), jnp.float32),
        jnp.zeros((local_rows, head_count, DH), jnp.float32),
    )
    members = lax.axis_size("ctx")
    my_index = lax.axis_index("ctx")
    block_rows = key_rows.shape[0]
    stacked = jnp.stack([key_rows, hyena_out])
    first_state = fold(initial, (key_rows, hyena_out), my_index * block_rows)

    def chain_step(step_index, carried):
        current, held = carried
        held = passed_along(held, "ctx", 1)
        anchor = (my_index - 1 - step_index) % members
        current = fold(current, (held[0], held[1]), anchor * block_rows)
        return (current, held)

    softmax_state, last_held = lax.fori_loop(0, members - 1, chain_step, (first_state, stacked))
    final_max, final_sum, weighted = softmax_state
    return (weighted / final_sum[:, :, None]).reshape(local_rows, channels).astype(jnp.bfloat16)


def shards(inner_gate, outer_gate, signal, filters, bypass, query_rows, key_rows):
    local_rows, channels = signal.shape
    members = lax.axis_size("ctx")
    my_index = lax.axis_index("ctx")
    product = (inner_gate.astype(jnp.float32) * signal.astype(jnp.float32)).astype(jnp.bfloat16)
    left_rim = passed_along_2(product[local_rows - (TAPS - 1) :], "ctx", 1)
    extended = jnp.concatenate([left_rim, product], axis=0).astype(jnp.float32)
    group_count = filters.shape[0]
    group_width = channels // group_count
    window_rows = 2 * TAPS - 1
    flipped = filters[:, ::-1]
    padded = jnp.concatenate([flipped, jnp.zeros((group_count, TAPS), jnp.float32)], axis=1)
    banded = jnp.tile(padded, (1, TAPS))[:, : TAPS * window_rows].reshape(
        group_count, TAPS, window_rows
    )
    block_count = local_rows // TAPS
    windows = jnp.stack([extended])
    windows = windows.reshape(block_count, window_rows, group_count, group_width)
    convolved = jnp.einsum(
        "gtj,bjgc->btgc", banded, windows, precision=lax.Precision.HIGHEST
    ).reshape(local_rows, channels)
    hyena_out = (
        outer_gate.astype(jnp.float32) * (convolved + bypass[None, :] * product.astype(jnp.float32))
    ).astype(jnp.bfloat16)
    per_source = local_rows // members
    spread = lax.all_to_all(
        query_rows.reshape(per_source, members, channels),
        "ctx",
        split_axis=1,
        concat_axis=1,
        tiled=True,
    )
    source = jnp.arange(members, dtype=jnp.int32)[None, :]
    offset = jnp.arange(per_source, dtype=jnp.int32)[:, None]
    query_pos = (source * local_rows + offset * members + my_index).reshape(local_rows)
    local_queries = spread.reshape(local_rows, channels)
    attended = attend(local_queries, query_pos, key_rows, hyena_out)
    returned = lax.all_to_all(
        attended.reshape(per_source, members, channels),
        "ctx",
        split_axis=1,
        concat_axis=1,
        tiled=True,
    )
    attended = returned.reshape(local_rows, channels)
    return (hyena_out, attended)


def solution(mesh):
    placed = (
        P(("dp", "ctx"), None),
        P(("dp", "ctx"), None),
        P(("dp", "ctx"), None),
        P(),
        P(),
        P(("dp", "ctx"), None),
        P(("dp", "ctx"), None),
    )
    return jax.shard_map(
        shards,
        mesh=mesh,
        in_specs=placed,
        out_specs=(P(("dp", "ctx"), None), P(("dp", "ctx"), None)),
        check_vma=False,
    )
```

profile of v0, /device:TPU:56, one launch (start us, length us, event | category | flops | bytes accessed | tf_op | source)
XLA Modules:
  0.0 632.5 jit_solution(6121067167949745488)
XLA Ops:
  7.1 12.9 %all-to-all-start = ((bf16[4,32,1024]{2,0,1:T(4,128)(2,1)}), bf16[4,32,1024]{2,0,1:T(4,128)(2,1)S(1)}, u32[]{:S(2)}, u32[]{:S(2)}) async-start(bf16[4,32,1024]{2,0,1:T(4,128)(2,1)} %copy.49), calls=%async_computation | async-start | bytes 524288 | tf_op jit(solution)/shard_map/all_to_all | solution.py:116
  30.0 15.9 %reshape.132 = f32[64,128,255]{2,1,0:T(8,128)} reshape(f32[64,32640]{1,0:T(8,128)} %slice.27) | data formatting | bytes 16711680 | tf_op jit(solution)/shard_map/reshape | solution.py:103
  58.6 554.3 %while.22 = (s32[]{:T(128)}, f32[128,8]{0,1:T(8,128)S(1)}, f32[128,8]{0,1:T(8,128)S(1)}, f32[128,8,128]{2,0,1:T(8,128)S(1)}, bf16[2,128,1024]{1,2,0:T(8,128)(2,1...) while((s32[]{:T(128)}, f32[128,8]{0,1:T(8,128)S(1)}, ...), condition=%wide.region_10.11_spmd.clone, body=%wide.region_5.10_spmd.clone.sunk | while | flops 68569488 | bytes 7736928 | solution.py:86
  62.9 14.0 %collective-permute-done = bf16[2,128,1024]{1,2,0:T(8,128)(2,1)S(1)} collective-permute-done((bf16[2,128,1024]{1,2,0:T(8,128)(2,1)S(1)}, bf16[2,128,1024]{1,2,0:T(8,128)(2,1)S(1)}, u32[]{:S(2)}, u32[]{:S(2)}) %collective-permute-start) | collective-permute-done | bytes 524320 | tf_op jit(solution)/shard_map/while/body/eval_jaxpr/ppermute | solution.py:13
  80.8 14.9 %collective-permute-done = bf16[2,128,1024]{1,2,0:T(8,128)(2,1)S(1)} collective-permute-done((bf16[2,128,1024]{1,2,0:T(8,128)(2,1)S(1)}, bf16[2,128,1024]{1,2,0:T(8,128)(2,1)S(1)}, u32[]{:S(2)}, u32[]{:S(2)}) %collective-permute-start) | collective-permute-done | bytes 524320 | tf_op jit(solution)/shard_map/while/body/eval_jaxpr/ppermute | solution.py:13
  99.5 14.0 %collective-permute-done = bf16[2,128,1024]{1,2,0:T(8,128)(2,1)S(1)} collective-permute-done((bf16[2,128,1024]{1,2,0:T(8,128)(2,1)S(1)}, bf16[2,128,1024]{1,2,0:T(8,128)(2,1)S(1)}, u32[]{:S(2)}, u32[]{:S(2)}) %collective-permute-start) | collective-permute-done | bytes 524320 | tf_op jit(solution)/shard_map/while/body/eval_jaxpr/ppermute | solution.py:13
  117.5 13.2 %collective-permute-done = bf16[2,128,1024]{1,2,0:T(8,128)(2,1)S(1)} collective-permute-done((bf16[2,128,1024]{1,2,0:T(8,128)(2,1)S(1)}, bf16[2,128,1024]{1,2,0:T(8,128)(2,1)S(1)}, u32[]{:S(2)}, u32[]{:S(2)}) %collective-permute-start) | collective-permute-done | bytes 524320 | tf_op jit(solution)/shard_map/while/body/eval_jaxpr/ppermute | solution.py:13
  134.5 12.3 %collective-permute-done = bf16[2,128,1024]{1,2,0:T(8,128)(2,1)S(1)} collective-permute-done((bf16[2,128,1024]{1,2,0:T(8,128)(2,1)S(1)}, bf16[2,128,1024]{1,2,0:T(8,128)(2,1)S(1)}, u32[]{:S(2)}, u32[]{:S(2)}) %collective-permute-start) | collective-permute-done | bytes 524320 | tf_op jit(solution)/shard_map/while/body/eval_jaxpr/ppermute | solution.py:13
  150.7 11.8 %collective-permute-done = bf16[2,128,1024]{1,2,0:T(8,128)(2,1)S(1)} collective-permute-done((bf16[2,128,1024]{1,2,0:T(8,128)(2,1)S(1)}, bf16[2,128,1024]{1,2,0:T(8,128)(2,1)S(1)}, u32[]{:S(2)}, u32[]{:S(2)}) %collective-permute-start) | collective-permute-done | bytes 524320 | tf_op jit(solution)/shard_map/while/body/eval_jaxpr/ppermute | solution.py:13
  166.4 11.8 %collective-permute-done = bf16[2,128,1024]{1,2,0:T(8,128)(2,1)S(1)} collective-permute-done((bf16[2,128,1024]{1,2,0:T(8,128)(2,1)S(1)}, bf16[2,128,1024]{1,2,0:T(8,128)(2,1)S(1)}, u32[]{:S(2)}, u32[]{:S(2)}) %collective-permute-start) | collective-permute-done | bytes 524320 | tf_op jit(solution)/shard_map/while/body/eval_jaxpr/ppermute | solution.py:13
  182.1 11.8 %collective-permute-done = bf16[2,128,1024]{1,2,0:T(8,128)(2,1)S(1)} collective-permute-done((bf16[2,128,1024]{1,2,0:T(8,128)(2,1)S(1)}, bf16[2,128,1024]{1,2,0:T(8,128)(2,1)S(1)}, u32[]{:S(2)}, u32[]{:S(2)}) %collective-permute-start) | collective-permute-done | bytes 524320 | tf_op jit(solution)/shard_map/while/body/eval_jaxpr/ppermute | solution.py:13
  197.8 12.3 %collective-permute-done = bf16[2,128,1024]{1,2,0:T(8,128)(2,1)S(1)} collective-permute-done((bf16[2,128,1024]{1,2,0:T(8,128)(2,1)S(1)}, bf16[2,128,1024]{1,2,0:T(8,128)(2,1)S(1)}, u32[]{:S(2)}, u32[]{:S(2)}) %collective-permute-start) | collective-permute-done | bytes 524320 | tf_op jit(solution)/shard_map/while/body/eval_jaxpr/ppermute | solution.py:13
  214.1 13.5 %collective-permute-done = bf16[2,128,1024]{1,2,0:T(8,128)(2,1)S(1)} collective-permute-done((bf16[2,128,1024]{1,2,0:T(8,128)(2,1)S(1)}, bf16[2,128,1024]{1,2,0:T(8,128)(2,1)S(1)}, u32[]{:S(2)}, u32[]{:S(2)}) %collective-permute-start) | collective-permute-done | bytes 524320 | tf_op jit(solution)/shard_map/while/body/eval_jaxpr/ppermute | solution.py:13
  231.4 14.6 %collective-permute-done = bf16[2,128,1024]{1,2,0:T(8,128)(2,1)S(1)} collective-permute-done((bf16[2,128,1024]{1,2,0:T(8,128)(2,1)S(1)}, bf16[2,128,1024]{1,2,0:T(8,128)(2,1)S(1)}, u32[]{:S(2)}, u32[]{:S(2)}) %collective-permute-start) | collective-permute-done | bytes 524320 | tf_op jit(solution)/shard_map/while/body/eval_jaxpr/ppermute | solution.py:13
  249.9 15.8 %collective-permute-done = bf16[2,128,1024]{1,2,0:T(8,128)(2,1)S(1)} collective-permute-done((bf16[2,128,1024]{1,2,0:T(8,128)(2,1)S(1)}, bf16[2,128,1024]{1,2,0:T(8,128)(2,1)S(1)}, u32[]{:S(2)}, u32[]{:S(2)}) %collective-permute-start) | collective-permute-done | bytes 524320 | tf_op jit(solution)/shard_map/while/body/eval_jaxpr/ppermute | solution.py:13
  269.6 16.9 %collective-permute-done = bf16[2,128,1024]{1,2,0:T(8,128)(2,1)S(1)} collective-permute-done((bf16[2,128,1024]{1,2,0:T(8,128)(2,1)S(1)}, bf16[2,128,1024]{1,2,0:T(8,128)(2,1)S(1)}, u32[]{:S(2)}, u32[]{:S(2)}) %collective-permute-start) | collective-permute-done | bytes 524320 | tf_op jit(solution)/shard_map/while/body/eval_jaxpr/ppermute | solution.py:13
  290.4 16.8 %collective-permute-done = bf16[2,128,1024]{1,2,0:T(8,128)(2,1)S(1)} collective-permute-done((bf16[2,128,1024]{1,2,0:T(8,128)(2,1)S(1)}, bf16[2,128,1024]{1,2,0:T(8,128)(2,1)S(1)}, u32[]{:S(2)}, u32[]{:S(2)}) %collective-permute-start) | collective-permute-done | bytes 524320 | tf_op jit(solution)/shard_map/while/body/eval_jaxpr/ppermute | solution.py:13
  311.1 16.0 %collective-permute-done = bf16[2,128,1024]{1,2,0:T(8,128)(2,1)S(1)} collective-permute-done((bf16[2,128,1024]{1,2,0:T(8,128)(2,1)S(1)}, bf16[2,128,1024]{1,2,0:T(8,128)(2,1)S(1)}, u32[]{:S(2)}, u32[]{:S(2)}) %collective-permute-start) | collective-permute-done | bytes 524320 | tf_op jit(solution)/shard_map/while/body/eval_jaxpr/ppermute | solution.py:13
  330.9 15.1 %collective-permute-done = bf16[2,128,1024]{1,2,0:T(8,128)(2,1)S(1)} collective-permute-done((bf16[2,128,1024]{1,2,0:T(8,128)(2,1)S(1)}, bf16[2,128,1024]{1,2,0:T(8,128)(2,1)S(1)}, u32[]{:S(2)}, u32[]{:S(2)}) %collective-permute-start) | collective-permute-done | bytes 524320 | tf_op jit(solution)/shard_map/while/body/eval_jaxpr/ppermute | solution.py:13
  349.9 14.3 %collective-permute-done = bf16[2,128,1024]{1,2,0:T(8,128)(2,1)S(1)} collective-permute-done((bf16[2,128,1024]{1,2,0:T(8,128)(2,1)S(1)}, bf16[2,128,1024]{1,2,0:T(8,128)(2,1)S(1)}, u32[]{:S(2)}, u32[]{:S(2)}) %collective-permute-start) | collective-permute-done | bytes 524320 | tf_op jit(solution)/shard_map/while/body/eval_jaxpr/ppermute | solution.py:13
  368.1 13.4 %collective-permute-done = bf16[2,128,1024]{1,2,0:T(8,128)(2,1)S(1)} collective-permute-done((bf16[2,128,1024]{1,2,0:T(8,128)(2,1)S(1)}, bf16[2,128,1024]{1,2,0:T(8,128)(2,1)S(1)}, u32[]{:S(2)}, u32[]{:S(2)}) %collective-permute-start) | collective-permute-done | bytes 524320 | tf_op jit(solution)/shard_map/while/body/eval_jaxpr/ppermute | solution.py:13
  385.4 12.5 %collective-permute-done = bf16[2,128,1024]{1,2,0:T(8,128)(2,1)S(1)} collective-permute-done((bf16[2,128,1024]{1,2,0:T(8,128)(2,1)S(1)}, bf16[2,128,1024]{1,2,0:T(8,128)(2,1)S(1)}, u32[]{:S(2)}, u32[]{:S(2)}) %collective-permute-start) | collective-permute-done | bytes 524320 | tf_op jit(solution)/shard_map/while/body/eval_jaxpr/ppermute | solution.py:13
  401.8 11.8 %collective-permute-done = bf16[2,128,1024]{1,2,0:T(8,128)(2,1)S(1)} collective-permute-done((bf16[2,128,1024]{1,2,0:T(8,128)(2,1)S(1)}, bf16[2,128,1024]{1,2,0:T(8,128)(2,1)S(1)}, u32[]{:S(2)}, u32[]{:S(2)}) %collective-permute-start) | collective-permute-done | bytes 524320 | tf_op jit(solution)/shard_map/while/body/eval_jaxpr/ppermute | solution.py:13
  449.0 12.1 %collective-permute-done = bf16[2,128,1024]{1,2,0:T(8,128)(2,1)S(1)} collective-permute-done((bf16[2,128,1024]{1,2,0:T(8,128)(2,1)S(1)}, bf16[2,128,1024]{1,2,0:T(8,128)(2,1)S(1)}, u32[]{:S(2)}, u32[]{:S(2)}) %collective-permute-start) | collective-permute-done | bytes 524320 | tf_op jit(solution)/shard_map/while/body/eval_jaxpr/ppermute | solution.py:13
  464.9 13.2 %collective-permute-done = bf16[2,128,1024]{1,2,0:T(8,128)(2,1)S(1)} collective-permute-done((bf16[2,128,1024]{1,2,0:T(8,128)(2,1)S(1)}, bf16[2,128,1024]{1,2,0:T(8,128)(2,1)S(1)}, u32[]{:S(2)}, u32[]{:S(2)}) %collective-permute-start) | collective-permute-done | bytes 524320 | tf_op jit(solution)/shard_map/while/body/eval_jaxpr/ppermute | solution.py:13
  482.1 14.4 %collective-permute-done = bf16[2,128,1024]{1,2,0:T(8,128)(2,1)S(1)} collective-permute-done((bf16[2,128,1024]{1,2,0:T(8,128)(2,1)S(1)}, bf16[2,128,1024]{1,2,0:T(8,128)(2,1)S(1)}, u32[]{:S(2)}, u32[]{:S(2)}) %collective-permute-start) | collective-permute-done | bytes 524320 | tf_op jit(solution)/shard_map/while/body/eval_jaxpr/ppermute | solution.py:13
  500.4 15.5 %collective-permute-done = bf16[2,128,1024]{1,2,0:T(8,128)(2,1)S(1)} collective-permute-done((bf16[2,128,1024]{1,2,0:T(8,128)(2,1)S(1)}, bf16[2,128,1024]{1,2,0:T(8,128)(2,1)S(1)}, u32[]{:S(2)}, u32[]{:S(2)}) %collective-permute-start) | collective-permute-done | bytes 524320 | tf_op jit(solution)/shard_map/while/body/eval_jaxpr/ppermute | solution.py:13
  519.8 16.7 %collective-permute-done = bf16[2,128,1024]{1,2,0:T(8,128)(2,1)S(1)} collective-permute-done((bf16[2,128,1024]{1,2,0:T(8,128)(2,1)S(1)}, bf16[2,128,1024]{1,2,0:T(8,128)(2,1)S(1)}, u32[]{:S(2)}, u32[]{:S(2)}) %collective-permute-start) | collective-permute-done | bytes 524320 | tf_op jit(solution)/shard_map/while/body/eval_jaxpr/ppermute | solution.py:13
  540.4 17.0 %collective-permute-done = bf16[2,128,1024]{1,2,0:T(8,128)(2,1)S(1)} collective-permute-done((bf16[2,128,1024]{1,2,0:T(8,128)(2,1)S(1)}, bf16[2,128,1024]{1,2,0:T(8,128)(2,1)S(1)}, u32[]{:S(2)}, u32[]{:S(2)}) %collective-permute-start) | collective-permute-done | bytes 524320 | tf_op jit(solution)/shard_map/while/body/eval_jaxpr/ppermute | solution.py:13
  561.3 16.2 %collective-permute-done = bf16[2,128,1024]{1,2,0:T(8,128)(2,1)S(1)} collective-permute-done((bf16[2,128,1024]{1,2,0:T(8,128)(2,1)S(1)}, bf16[2,128,1024]{1,2,0:T(8,128)(2,1)S(1)}, u32[]{:S(2)}, u32[]{:S(2)}) %collective-permute-start) | collective-permute-done | bytes 524320 | tf_op jit(solution)/shard_map/while/body/eval_jaxpr/ppermute | solution.py:13
  581.4 14.5 %collective-permute-done = bf16[2,128,1024]{1,2,0:T(8,128)(2,1)S(1)} collective-permute-done((bf16[2,128,1024]{1,2,0:T(8,128)(2,1)S(1)}, bf16[2,128,1024]{1,2,0:T(8,128)(2,1)S(1)}, u32[]{:S(2)}, u32[]{:S(2)}) %collective-permute-start) | collective-permute-done | bytes 524320 | tf_op jit(solution)/shard_map/while/body/eval_jaxpr/ppermute | solution.py:13
  613.6 18.1 %all_to_all.10 = bf16[4,32,1024]{2,0,1:T(4,128)(2,1)S(1)} all-to-all(bf16[4,32,1024]{2,0,1:T(4,128)(2,1)S(1)} %copy.55), channel_id=1, replica_groups=mesh['dp'=16,'ctx'=32] {'ctx'}, dimensions={1} | all-to-all | bytes 524288 | tf_op jit(solution)/shard_map/all_to_all | solution.py:128
  (481 shorter events, 205.1 us)
Async XLA Ops:
  1.8 45.5 %collective-permute-start.1 = (bf16[127,1024]{1,0:T(8,128)(2,1)S(1)}, bf16[127,1024]{1,0:T(8,128)(2,1)S(1)}, u32[]{:S(2)}, u32[]{:S(2)}) collective-permute-start(bf16[127,1024]{1,0:T(8,128)(2,1)S(1)} %slice.26), channel_id=1, source_target_pairs={{0,1},{1,2},{2,3},{3,4},{4,5},{5,6},{6,7},{7,8},{8,9},{9,10},{10,1... | collective-permute-start | bytes 780296 | tf_op jit(solution)/shard_map/ppermute | solution.py:19
  7.1 49.2 %all-to-all-start = ((bf16[4,32,1024]{2,0,1:T(4,128)(2,1)}), bf16[4,32,1024]{2,0,1:T(4,128)(2,1)S(1)}, u32[]{:S(2)}, u32[]{:S(2)}) async-start(bf16[4,32,1024]{2,0,1:T(4,128)(2,1)} %copy.49), calls=%async_computation | async-start | bytes 524288 | tf_op jit(solution)/shard_map/all_to_all | solution.py:116
  58.6 18.3 %collective-permute-start = (bf16[2,128,1024]{1,2,0:T(8,128)(2,1)S(1)}, bf16[2,128,1024]{1,2,0:T(8,128)(2,1)S(1)}, u32[]{:S(2)}, u32[]{:S(2)}) collective-permute-start(bf16[2,128,1024]{1,2,0:T(8,128)(2,1)S(1)} %get-tuple-element.522), channel_id=1, source_target_pairs={{0,1},{1,2},{2,3},{3,4},{4,5},{5,6},{6,7},{7,8},{8,9},{9,10},{10,1... | collective-permute-start | bytes 1572872 | tf_op jit(solution)/shard_map/while/body/eval_jaxpr/ppermute | solution.py:13
  78.2 17.4 %collective-permute-start = (bf16[2,128,1024]{1,2,0:T(8,128)(2,1)S(1)}, bf16[2,128,1024]{1,2,0:T(8,128)(2,1)S(1)}, u32[]{:S(2)}, u32[]{:S(2)}) collective-permute-start(bf16[2,128,1024]{1,2,0:T(8,128)(2,1)S(1)} %get-tuple-element.522), channel_id=1, source_target_pairs={{0,1},{1,2},{2,3},{3,4},{4,5},{5,6},{6,7},{7,8},{8,9},{9,10},{10,1... | collective-permute-start | bytes 1572872 | tf_op jit(solution)/shard_map/while/body/eval_jaxpr/ppermute | solution.py:13
  97.0 16.6 %collective-permute-start = (bf16[2,128,1024]{1,2,0:T(8,128)(2,1)S(1)}, bf16[2,128,1024]{1,2,0:T(8,128)(2,1)S(1)}, u32[]{:S(2)}, u32[]{:S(2)}) collective-permute-start(bf16[2,128,1024]{1,2,0:T(8,128)(2,1)S(1)} %get-tuple-element.522), channel_id=1, source_target_pairs={{0,1},{1,2},{2,3},{3,4},{4,5},{5,6},{6,7},{7,8},{8,9},{9,10},{10,1... | collective-permute-start | bytes 1572872 | tf_op jit(solution)/shard_map/while/body/eval_jaxpr/ppermute | solution.py:13
  114.9 15.7 %collective-permute-start = (bf16[2,128,1024]{1,2,0:T(8,128)(2,1)S(1)}, bf16[2,128,1024]{1,2,0:T(8,128)(2,1)S(1)}, u32[]{:S(2)}, u32[]{:S(2)}) collective-permute-start(bf16[2,128,1024]{1,2,0:T(8,128)(2,1)S(1)} %get-tuple-element.522), channel_id=1, source_target_pairs={{0,1},{1,2},{2,3},{3,4},{4,5},{5,6},{6,7},{7,8},{8,9},{9,10},{10,1... | collective-permute-start | bytes 1572872 | tf_op jit(solution)/shard_map/while/body/eval_jaxpr/ppermute | solution.py:13
  131.9 14.9 %collective-permute-start = (bf16[2,128,1024]{1,2,0:T(8,128)(2,1)S(1)}, bf16[2,128,1024]{1,2,0:T(8,128)(2,1)S(1)}, u32[]{:S(2)}, u32[]{:S(2)}) collective-permute-start(bf16[2,128,1024]{1,2,0:T(8,128)(2,1)S(1)} %get-tuple-element.522), channel_id=1, source_target_pairs={{0,1},{1,2},{2,3},{3,4},{4,5},{5,6},{6,7},{7,8},{8,9},{9,10},{10,1... | collective-permute-start | bytes 1572872 | tf_op jit(solution)/shard_map/while/body/eval_jaxpr/ppermute | solution.py:13
  148.1 14.4 %collective-permute-start = (bf16[2,128,1024]{1,2,0:T(8,128)(2,1)S(1)}, bf16[2,128,1024]{1,2,0:T(8,128)(2,1)S(1)}, u32[]{:S(2)}, u32[]{:S(2)}) collective-permute-start(bf16[2,128,1024]{1,2,0:T(8,128)(2,1)S(1)} %get-tuple-element.522), channel_id=1, source_target_pairs={{0,1},{1,2},{2,3},{3,4},{4,5},{5,6},{6,7},{7,8},{8,9},{9,10},{10,1... | collective-permute-start | bytes 1572872 | tf_op jit(solution)/shard_map/while/body/eval_jaxpr/ppermute | solution.py:13
  163.8 14.4 %collective-permute-start = (bf16[2,128,1024]{1,2,0:T(8,128)(2,1)S(1)}, bf16[2,128,1024]{1,2,0:T(8,128)(2,1)S(1)}, u32[]{:S(2)}, u32[]{:S(2)}) collective-permute-start(bf16[2,128,1024]{1,2,0:T(8,128)(2,1)S(1)} %get-tuple-element.522), channel_id=1, source_target_pairs={{0,1},{1,2},{2,3},{3,4},{4,5},{5,6},{6,7},{7,8},{8,9},{9,10},{10,1... | collective-permute-start | bytes 1572872 | tf_op jit(solution)/shard_map/while/body/eval_jaxpr/ppermute | solution.py:13
  179.6 14.4 %collective-permute-start = (bf16[2,128,1024]{1,2,0:T(8,128)(2,1)S(1)}, bf16[2,128,1024]{1,2,0:T(8,128)(2,1)S(1)}, u32[]{:S(2)}, u32[]{:S(2)}) collective-permute-start(bf16[2,128,1024]{1,2,0:T(8,128)(2,1)S(1)} %get-tuple-element.522), channel_id=1, source_target_pairs={{0,1},{1,2},{2,3},{3,4},{4,5},{5,6},{6,7},{7,8},{8,9},{9,10},{10,1... | collective-permute-start | bytes 1572872 | tf_op jit(solution)/shard_map/while/body/eval_jaxpr/ppermute | solution.py:13
  195.3 14.9 %collective-permute-start = (bf16[2,128,1024]{1,2,0:T(8,128)(2,1)S(1)}, bf16[2,128,1024]{1,2,0:T(8,128)(2,1)S(1)}, u32[]{:S(2)}, u32[]{:S(2)}) collective-permute-start(bf16[2,128,1024]{1,2,0:T(8,128)(2,1)S(1)} %get-tuple-element.522), channel_id=1, source_target_pairs={{0,1},{1,2},{2,3},{3,4},{4,5},{5,6},{6,7},{7,8},{8,9},{9,10},{10,1... | collective-permute-start | bytes 1572872 | tf_op jit(solution)/shard_map/while/body/eval_jaxpr/ppermute | solution.py:13
  211.5 16.0 %collective-permute-start = (bf16[2,128,1024]{1,2,0:T(8,128)(2,1)S(1)}, bf16[2,128,1024]{1,2,0:T(8,128)(2,1)S(1)}, u32[]{:S(2)}, u32[]{:S(2)}) collective-permute-start(bf16[2,128,1024]{1,2,0:T(8,128)(2,1)S(1)} %get-tuple-element.522), channel_id=1, source_target_pairs={{0,1},{1,2},{2,3},{3,4},{4,5},{5,6},{6,7},{7,8},{8,9},{9,10},{10,1... | collective-permute-start | bytes 1572872 | tf_op jit(solution)/shard_map/while/body/eval_jaxpr/ppermute | solution.py:13
  228.8 17.2 %collective-permute-start = (bf16[2,128,1024]{1,2,0:T(8,128)(2,1)S(1)}, bf16[2,128,1024]{1,2,0:T(8,128)(2,1)S(1)}, u32[]{:S(2)}, u32[]{:S(2)}) collective-permute-start(bf16[2,128,1024]{1,2,0:T(8,128)(2,1)S(1)} %get-tuple-element.522), channel_id=1, source_target_pairs={{0,1},{1,2},{2,3},{3,4},{4,5},{5,6},{6,7},{7,8},{8,9},{9,10},{10,1... | collective-permute-start | bytes 1572872 | tf_op jit(solution)/shard_map/while/body/eval_jaxpr/ppermute | solution.py:13
  247.3 18.3 %collective-permute-start = (bf16[2,128,1024]{1,2,0:T(8,128)(2,1)S(1)}, bf16[2,128,1024]{1,2,0:T(8,128)(2,1)S(1)}, u32[]{:S(2)}, u32[]{:S(2)}) collective-permute-start(bf16[2,128,1024]{1,2,0:T(8,128)(2,1)S(1)} %get-tuple-element.522), channel_id=1, source_target_pairs={{0,1},{1,2},{2,3},{3,4},{4,5},{5,6},{6,7},{7,8},{8,9},{9,10},{10,1... | collective-permute-start | bytes 1572872 | tf_op jit(solution)/shard_map/while/body/eval_jaxpr/ppermute | solution.py:13
  267.0 19.5 %collective-permute-start = (bf16[2,128,1024]{1,2,0:T(8,128)(2,1)S(1)}, bf16[2,128,1024]{1,2,0:T(8,128)(2,1)S(1)}, u32[]{:S(2)}, u32[]{:S(2)}) collective-permute-start(bf16[2,128,1024]{1,2,0:T(8,128)(2,1)S(1)} %get-tuple-element.522), channel_id=1, source_target_pairs={{0,1},{1,2},{2,3},{3,4},{4,5},{5,6},{6,7},{7,8},{8,9},{9,10},{10,1... | collective-permute-start | bytes 1572872 | tf_op jit(solution)/shard_map/while/body/eval_jaxpr/ppermute | solution.py:13
  287.8 19.4 %collective-permute-start = (bf16[2,128,1024]{1,2,0:T(8,128)(2,1)S(1)}, bf16[2,128,1024]{1,2,0:T(8,128)(2,1)S(1)}, u32[]{:S(2)}, u32[]{:S(2)}) collective-permute-start(bf16[2,128,1024]{1,2,0:T(8,128)(2,1)S(1)} %get-tuple-element.522), channel_id=1, source_target_pairs={{0,1},{1,2},{2,3},{3,4},{4,5},{5,6},{6,7},{7,8},{8,9},{9,10},{10,1... | collective-permute-start | bytes 1572872 | tf_op jit(solution)/shard_map/while/body/eval_jaxpr/ppermute | solution.py:13
  308.5 18.5 %collective-permute-start = (bf16[2,128,1024]{1,2,0:T(8,128)(2,1)S(1)}, bf16[2,128,1024]{1,2,0:T(8,128)(2,1)S(1)}, u32[]{:S(2)}, u32[]{:S(2)}) collective-permute-start(bf16[2,128,1024]{1,2,0:T(8,128)(2,1)S(1)} %get-tuple-element.522), channel_id=1, source_target_pairs={{0,1},{1,2},{2,3},{3,4},{4,5},{5,6},{6,7},{7,8},{8,9},{9,10},{10,1... | collective-permute-start | bytes 1572872 | tf_op jit(solution)/shard_map/while/body/eval_jaxpr/ppermute | solution.py:13
  328.4 17.7 %collective-permute-start = (bf16[2,128,1024]{1,2,0:T(8,128)(2,1)S(1)}, bf16[2,128,1024]{1,2,0:T(8,128)(2,1)S(1)}, u32[]{:S(2)}, u32[]{:S(2)}) collective-permute-start(bf16[2,128,1024]{1,2,0:T(8,128)(2,1)S(1)} %get-tuple-element.522), channel_id=1, source_target_pairs={{0,1},{1,2},{2,3},{3,4},{4,5},{5,6},{6,7},{7,8},{8,9},{9,10},{10,1... | collective-permute-start | bytes 1572872 | tf_op jit(solution)/shard_map/while/body/eval_jaxpr/ppermute | solution.py:13
  347.4 16.8 %collective-permute-start = (bf16[2,128,1024]{1,2,0:T(8,128)(2,1)S(1)}, bf16[2,128,1024]{1,2,0:T(8,128)(2,1)S(1)}, u32[]{:S(2)}, u32[]{:S(2)}) collective-permute-start(bf16[2,128,1024]{1,2,0:T(8,128)(2,1)S(1)} %get-tuple-element.522), channel_id=1, source_target_pairs={{0,1},{1,2},{2,3},{3,4},{4,5},{5,6},{6,7},{7,8},{8,9},{9,10},{10,1... | collective-permute-start | bytes 1572872 | tf_op jit(solution)/shard_map/while/body/eval_jaxpr/ppermute | solution.py:13
  365.5 16.0 %collective-permute-start = (bf16[2,128,1024]{1,2,0:T(8,128)(2,1)S(1)}, bf16[2,128,1024]{1,2,0:T(8,128)(2,1)S(1)}, u32[]{:S(2)}, u32[]{:S(2)}) collective-permute-start(bf16[2,128,1024]{1,2,0:T(8,128)(2,1)S(1)} %get-tuple-element.522), channel_id=1, source_target_pairs={{0,1},{1,2},{2,3},{3,4},{4,5},{5,6},{6,7},{7,8},{8,9},{9,10},{10,1... | collective-permute-start | bytes 1572872 | tf_op jit(solution)/shard_map/while/body/eval_jaxpr/ppermute | solution.py:13
  382.8 15.1 %collective-permute-start = (bf16[2,128,1024]{1,2,0:T(8,128)(2,1)S(1)}, bf16[2,128,1024]{1,2,0:T(8,128)(2,1)S(1)}, u32[]{:S(2)}, u32[]{:S(2)}) collective-permute-start(bf16[2,128,1024]{1,2,0:T(8,128)(2,1)S(1)} %get-tuple-element.522), channel_id=1, source_target_pairs={{0,1},{1,2},{2,3},{3,4},{4,5},{5,6},{6,7},{7,8},{8,9},{9,10},{10,1... | collective-permute-start | bytes 1572872 | tf_op jit(solution)/shard_map/while/body/eval_jaxpr/ppermute | solution.py:13
  399.2 14.4 %collective-permute-start = (bf16[2,128,1024]{1,2,0:T(8,128)(2,1)S(1)}, bf16[2,128,1024]{1,2,0:T(8,128)(2,1)S(1)}, u32[]{:S(2)}, u32[]{:S(2)}) collective-permute-start(bf16[2,128,1024]{1,2,0:T(8,128)(2,1)S(1)} %get-tuple-element.522), channel_id=1, source_target_pairs={{0,1},{1,2},{2,3},{3,4},{4,5},{5,6},{6,7},{7,8},{8,9},{9,10},{10,1... | collective-permute-start | bytes 1572872 | tf_op jit(solution)/shard_map/while/body/eval_jaxpr/ppermute | solution.py:13
  415.0 14.4 %collective-permute-start = (bf16[2,128,1024]{1,2,0:T(8,128)(2,1)S(1)}, bf16[2,128,1024]{1,2,0:T(8,128)(2,1)S(1)}, u32[]{:S(2)}, u32[]{:S(2)}) collective-permute-start(bf16[2,128,1024]{1,2,0:T(8,128)(2,1)S(1)} %get-tuple-element.522), channel_id=1, source_target_pairs={{0,1},{1,2},{2,3},{3,4},{4,5},{5,6},{6,7},{7,8},{8,9},{9,10},{10,1... | collective-permute-start | bytes 1572872 | tf_op jit(solution)/shard_map/while/body/eval_jaxpr/ppermute | solution.py:13
  430.7 14.4 %collective-permute-start = (bf16[2,128,1024]{1,2,0:T(8,128)(2,1)S(1)}, bf16[2,128,1024]{1,2,0:T(8,128)(2,1)S(1)}, u32[]{:S(2)}, u32[]{:S(2)}) collective-permute-start(bf16[2,128,1024]{1,2,0:T(8,128)(2,1)S(1)} %get-tuple-element.522), channel_id=1, source_target_pairs={{0,1},{1,2},{2,3},{3,4},{4,5},{5,6},{6,7},{7,8},{8,9},{9,10},{10,1... | collective-permute-start | bytes 1572872 | tf_op jit(solution)/shard_map/while/body/eval_jaxpr/ppermute | solution.py:13
  446.4 14.7 %collective-permute-start = (bf16[2,128,1024]{1,2,0:T(8,128)(2,1)S(1)}, bf16[2,128,1024]{1,2,0:T(8,128)(2,1)S(1)}, u32[]{:S(2)}, u32[]{:S(2)}) collective-permute-start(bf16[2,128,1024]{1,2,0:T(8,128)(2,1)S(1)} %get-tuple-element.522), channel_id=1, source_target_pairs={{0,1},{1,2},{2,3},{3,4},{4,5},{5,6},{6,7},{7,8},{8,9},{9,10},{10,1... | collective-permute-start | bytes 1572872 | tf_op jit(solution)/shard_map/while/body/eval_jaxpr/ppermute | solution.py:13
  462.4 15.8 %collective-permute-start = (bf16[2,128,1024]{1,2,0:T(8,128)(2,1)S(1)}, bf16[2,128,1024]{1,2,0:T(8,128)(2,1)S(1)}, u32[]{:S(2)}, u32[]{:S(2)}) collective-permute-start(bf16[2,128,1024]{1,2,0:T(8,128)(2,1)S(1)} %get-tuple-element.522), channel_id=1, source_target_pairs={{0,1},{1,2},{2,3},{3,4},{4,5},{5,6},{6,7},{7,8},{8,9},{9,10},{10,1... | collective-permute-start | bytes 1572872 | tf_op jit(solution)/shard_map/while/body/eval_jaxpr/ppermute | solution.py:13
  479.5 17.0 %collective-permute-start = (bf16[2,128,1024]{1,2,0:T(8,128)(2,1)S(1)}, bf16[2,128,1024]{1,2,0:T(8,128)(2,1)S(1)}, u32[]{:S(2)}, u32[]{:S(2)}) collective-permute-start(bf16[2,128,1024]{1,2,0:T(8,128)(2,1)S(1)} %get-tuple-element.522), channel_id=1, source_target_pairs={{0,1},{1,2},{2,3},{3,4},{4,5},{5,6},{6,7},{7,8},{8,9},{9,10},{10,1... | collective-permute-start | bytes 1572872 | tf_op jit(solution)/shard_map/while/body/eval_jaxpr/ppermute | solution.py:13
  497.8 18.1 %collective-permute-start = (bf16[2,128,1024]{1,2,0:T(8,128)(2,1)S(1)}, bf16[2,128,1024]{1,2,0:T(8,128)(2,1)S(1)}, u32[]{:S(2)}, u32[]{:S(2)}) collective-permute-start(bf16[2,128,1024]{1,2,0:T(8,128)(2,1)S(1)} %get-tuple-element.522), channel_id=1, source_target_pairs={{0,1},{1,2},{2,3},{3,4},{4,5},{5,6},{6,7},{7,8},{8,9},{9,10},{10,1... | collective-permute-start | bytes 1572872 | tf_op jit(solution)/shard_map/while/body/eval_jaxpr/ppermute | solution.py:13
  517.2 19.3 %collective-permute-start = (bf16[2,128,1024]{1,2,0:T(8,128)(2,1)S(1)}, bf16[2,128,1024]{1,2,0:T(8,128)(2,1)S(1)}, u32[]{:S(2)}, u32[]{:S(2)}) collective-permute-start(bf16[2,128,1024]{1,2,0:T(8,128)(2,1)S(1)} %get-tuple-element.522), channel_id=1, source_target_pairs={{0,1},{1,2},{2,3},{3,4},{4,5},{5,6},{6,7},{7,8},{8,9},{9,10},{10,1... | collective-permute-start | bytes 1572872 | tf_op jit(solution)/shard_map/while/body/eval_jaxpr/ppermute | solution.py:13
  537.8 19.6 %collective-permute-start = (bf16[2,128,1024]{1,2,0:T(8,128)(2,1)S(1)}, bf16[2,128,1024]{1,2,0:T(8,128)(2,1)S(1)}, u32[]{:S(2)}, u32[]{:S(2)}) collective-permute-start(bf16[2,128,1024]{1,2,0:T(8,128)(2,1)S(1)} %get-tuple-element.522), channel_id=1, source_target_pairs={{0,1},{1,2},{2,3},{3,4},{4,5},{5,6},{6,7},{7,8},{8,9},{9,10},{10,1... | collective-permute-start | bytes 1572872 | tf_op jit(solution)/shard_map/while/body/eval_jaxpr/ppermute | solution.py:13
  558.7 18.8 %collective-permute-start = (bf16[2,128,1024]{1,2,0:T(8,128)(2,1)S(1)}, bf16[2,128,1024]{1,2,0:T(8,128)(2,1)S(1)}, u32[]{:S(2)}, u32[]{:S(2)}) collective-permute-start(bf16[2,128,1024]{1,2,0:T(8,128)(2,1)S(1)} %get-tuple-element.522), channel_id=1, source_target_pairs={{0,1},{1,2},{2,3},{3,4},{4,5},{5,6},{6,7},{7,8},{8,9},{9,10},{10,1... | collective-permute-start | bytes 1572872 | tf_op jit(solution)/shard_map/while/body/eval_jaxpr/ppermute | solution.py:13
  578.8 17.0 %collective-permute-start = (bf16[2,128,1024]{1,2,0:T(8,128)(2,1)S(1)}, bf16[2,128,1024]{1,2,0:T(8,128)(2,1)S(1)}, u32[]{:S(2)}, u32[]{:S(2)}) collective-permute-start(bf16[2,128,1024]{1,2,0:T(8,128)(2,1)S(1)} %get-tuple-element.522), channel_id=1, source_target_pairs={{0,1},{1,2},{2,3},{3,4},{4,5},{5,6},{6,7},{7,8},{8,9},{9,10},{10,1... | collective-permute-start | bytes 1572872 | tf_op jit(solution)/shard_map/while/body/eval_jaxpr/ppermute | solution.py:13
  (4 other events, 39.9 us)
where the time goes:
time: 634 us; the launch traced here: 632 us
  waiting for transfers between devices  432 us (68%)
  starting transfers between devices  77.6 us (12%)
  local copies, waits for them, and re-layouts  35 us (6%)
  matrix products  32.3 us (5%)
  loops' own time  23.1 us (4%)
  blocking collectives  18.1 us (3%)
  other arithmetic  13 us (2%)
    ppermute x31, waiting for transfers between devices, passed_along(): lax.ppermute(array, axis, [(i, (i + by) % devices) for i in range(devices)])  432 us
    ppermute x31, starting transfers between devices, passed_along(): lax.ppermute(array, axis, [(i, (i + by) % devices) for i in range(devices)])  61.3 us
    another operation x1, loops' own time, attend(): lax.fori_loop(0, members - 1, chain_step, (first_state, stacked))  21.4 us
    all_to_all x1, blocking collectives, shards(): lax.all_to_all(attended.reshape(per_source, members, channels), 'ctx', sp...  18.1 us
    reshape x1, local copies, waits for them, and re-layouts, shards(): jnp.tile(padded, (1, TAPS))[:, :TAPS * window_rows]  15.9 us
    dot_general x32, matrix products, update_block(): jnp.einsum('thp,phd->thd', weights.astype(jnp.bfloat16), value_heads, pre...  15 us
    all_to_all x1, starting transfers between devices, shards(): lax.all_to_all(query_rows.reshape(per_source, members, channels), 'ctx',...  12.9 us
  transfers between devices with their start and end apart: 33, of which 31 were waited for; matrix products, arithmetic and copies ran while one was open for 6% of the time, Pallas kernels for 0%

commit v1 on v0

--- a/solution.py
+++ b/solution.py
@@ -125,13 +125,13 @@
     query_pos = (source * local_rows + offset * members + my_index).reshape(local_rows)
     local_queries = spread.reshape(local_rows, channels)
     attended = attend(local_queries, query_pos, key_rows, hyena_out)
-    returned = lax.all_to_all(
-        attended.reshape(per_source, members, channels),
-        "ctx",
-        split_axis=1,
-        concat_axis=1,
-        tiled=True,
+    _process_domain = lambda block_in, axis_name: jnp.concatenate(
+        lax.all_to_all(
+            jnp.stack(jnp.split(block_in, lax.axis_size(axis_name), 1)), axis_name, 0, 0
+        ),
+        1,
     )
+    returned = _process_domain(attended.reshape(per_source, members, channels), "ctx")
     attended = returned.reshape(local_rows, channels)
     return (hyena_out, attended)
 

time: 634 us -> 634 us (level)
  no operation moved by 1% of the time
where the time goes in v1:
time: 634 us; the launch traced here: 632 us
  waiting for transfers between devices  432 us (68%)
  starting transfers between devices  77.6 us (12%)
  local copies, waits for them, and re-layouts  38 us (6%)
  matrix products  31.4 us (5%)
  loops' own time  23.3 us (4%)
  blocking collectives  18.1 us (3%)
  other arithmetic  10.6 us (2%)
    ppermute x31, waiting for transfers between devices, passed_along(): lax.ppermute(array, axis, [(i, (i + by) % devices) for i in range(devices)])  432 us
    ppermute x31, starting transfers between devices, passed_along(): lax.ppermute(array, axis, [(i, (i + by) % devices) for i in range(devices)])  61.3 us
    another operation x1, loops' own time, attend(): lax.fori_loop(0, members - 1, chain_step, (first_state, stacked))  21.7 us
    all_to_all x1, blocking collectives, shards(): lax.all_to_all(jnp.stack(jnp.split(block_in, lax.axis_size(axis_name), 1)...  18.1 us
    reshape x1, local copies, waits for them, and re-layouts, shards(): jnp.tile(padded, (1, TAPS))[:, :TAPS * window_rows]  16 us
    dot_general x32, matrix products, update_block(): jnp.einsum('thp,phd->thd', weights.astype(jnp.bfloat16), value_heads, pre...  14.1 us
    all_to_all x1, starting transfers between devices, shards(): lax.all_to_all(query_rows.reshape(per_source, members, channels), 'ctx',...  12.9 us
  transfers between devices with their start and end apart: 33, of which 31 were waited for; matrix products, arithmetic and copies ran while one was open for 6% of the time, Pallas kernels for 0%

profile of v1, /device:TPU:56, one launch (start us, length us, event | category | flops | bytes accessed | tf_op | source)
XLA Modules:
  0.0 632.3 jit_solution(8170904308298449261)
XLA Ops:
  8.4 12.9 %all-to-all-start = ((bf16[4,32,1024]{2,0,1:T(4,128)(2,1)}), bf16[4,32,1024]{2,0,1:T(4,128)(2,1)S(1)}, u32[]{:S(2)}, u32[]{:S(2)}) async-start(bf16[4,32,1024]{2,0,1:T(4,128)(2,1)} %copy.926), calls=%async_computation | async-start | bytes 524288 | tf_op jit(solution)/shard_map/all_to_all | solution.py:116
  31.3 16.0 %reshape.132 = f32[64,128,255]{2,1,0:T(8,128)} reshape(f32[64,32640]{1,0:T(8,128)} %slice.27) | data formatting | bytes 16711680 | tf_op jit(solution)/shard_map/reshape | solution.py:103
  57.5 554.2 %while.22 = (s32[]{:T(128)}, f32[128,8]{0,1:T(8,128)S(1)}, f32[128,8]{0,1:T(8,128)S(1)}, f32[128,8,128]{2,0,1:T(8,128)S(1)}, bf16[2,128,1024]{1,2,0:T(8,128)(2,1...) while((s32[]{:T(128)}, f32[128,8]{0,1:T(8,128)S(1)}, ...), condition=%wide.region_10.11_spmd.clone, body=%wide.region_5.10_spmd.clone.sunk | while | flops 68569488 | bytes 7736928 | solution.py:86
  61.9 14.0 %collective-permute-done = bf16[2,128,1024]{1,2,0:T(8,128)(2,1)S(1)} collective-permute-done((bf16[2,128,1024]{1,2,0:T(8,128)(2,1)S(1)}, bf16[2,128,1024]{1,2,0:T(8,128)(2,1)S(1)}, u32[]{:S(2)}, u32[]{:S(2)}) %collective-permute-start) | collective-permute-done | bytes 524320 | tf_op jit(solution)/shard_map/while/body/eval_jaxpr/ppermute | solution.py:13
  79.8 14.9 %collective-permute-done = bf16[2,128,1024]{1,2,0:T(8,128)(2,1)S(1)} collective-permute-done((bf16[2,128,1024]{1,2,0:T(8,128)(2,1)S(1)}, bf16[2,128,1024]{1,2,0:T(8,128)(2,1)S(1)}, u32[]{:S(2)}, u32[]{:S(2)}) %collective-permute-start) | collective-permute-done | bytes 524320 | tf_op jit(solution)/shard_map/while/body/eval_jaxpr/ppermute | solution.py:13
  98.6 14.0 %collective-permute-done = bf16[2,128,1024]{1,2,0:T(8,128)(2,1)S(1)} collective-permute-done((bf16[2,128,1024]{1,2,0:T(8,128)(2,1)S(1)}, bf16[2,128,1024]{1,2,0:T(8,128)(2,1)S(1)}, u32[]{:S(2)}, u32[]{:S(2)}) %collective-permute-start) | collective-permute-done | bytes 524320 | tf_op jit(solution)/shard_map/while/body/eval_jaxpr/ppermute | solution.py:13
  116.5 13.2 %collective-permute-done = bf16[2,128,1024]{1,2,0:T(8,128)(2,1)S(1)} collective-permute-done((bf16[2,128,1024]{1,2,0:T(8,128)(2,1)S(1)}, bf16[2,128,1024]{1,2,0:T(8,128)(2,1)S(1)}, u32[]{:S(2)}, u32[]{:S(2)}) %collective-permute-start) | collective-permute-done | bytes 524320 | tf_op jit(solution)/shard_map/while/body/eval_jaxpr/ppermute | solution.py:13
  133.5 12.3 %collective-permute-done = bf16[2,128,1024]{1,2,0:T(8,128)(2,1)S(1)} collective-permute-done((bf16[2,128,1024]{1,2,0:T(8,128)(2,1)S(1)}, bf16[2,128,1024]{1,2,0:T(8,128)(2,1)S(1)}, u32[]{:S(2)}, u32[]{:S(2)}) %collective-permute-start) | collective-permute-done | bytes 524320 | tf_op jit(solution)/shard_map/while/body/eval_jaxpr/ppermute | solution.py:13
  149.7 11.8 %collective-permute-done = bf16[2,128,1024]{1,2,0:T(8,128)(2,1)S(1)} collective-permute-done((bf16[2,128,1024]{1,2,0:T(8,128)(2,1)S(1)}, bf16[2,128,1024]{1,2,0:T(8,128)(2,1)S(1)}, u32[]{:S(2)}, u32[]{:S(2)}) %collective-permute-start) | collective-permute-done | bytes 524320 | tf_op jit(solution)/shard_map/while/body/eval_jaxpr/ppermute | solution.py:13
  165.5 11.8 %collective-permute-done = bf16[2,128,1024]{1,2,0:T(8,128)(2,1)S(1)} collective-permute-done((bf16[2,128,1024]{1,2,0:T(8,128)(2,1)S(1)}, bf16[2,128,1024]{1,2,0:T(8,128)(2,1)S(1)}, u32[]{:S(2)}, u32[]{:S(2)}) %collective-permute-start) | collective-permute-done | bytes 524320 | tf_op jit(solution)/shard_map/while/body/eval_jaxpr/ppermute | solution.py:13
  181.2 11.8 %collective-permute-done = bf16[2,128,1024]{1,2,0:T(8,128)(2,1)S(1)} collective-permute-done((bf16[2,128,1024]{1,2,0:T(8,128)(2,1)S(1)}, bf16[2,128,1024]{1,2,0:T(8,128)(2,1)S(1)}, u32[]{:S(2)}, u32[]{:S(2)}) %collective-permute-start) | collective-permute-done | bytes 524320 | tf_op jit(solution)/shard_map/while/body/eval_jaxpr/ppermute | solution.py:13
  196.9 12.3 %collective-permute-done = bf16[2,128,1024]{1,2,0:T(8,128)(2,1)S(1)} collective-permute-done((bf16[2,128,1024]{1,2,0:T(8,128)(2,1)S(1)}, bf16[2,128,1024]{1,2,0:T(8,128)(2,1)S(1)}, u32[]{:S(2)}, u32[]{:S(2)}) %collective-permute-start) | collective-permute-done | bytes 524320 | tf_op jit(solution)/shard_map/while/body/eval_jaxpr/ppermute | solution.py:13
  213.1 13.5 %collective-permute-done = bf16[2,128,1024]{1,2,0:T(8,128)(2,1)S(1)} collective-permute-done((bf16[2,128,1024]{1,2,0:T(8,128)(2,1)S(1)}, bf16[2,128,1024]{1,2,0:T(8,128)(2,1)S(1)}, u32[]{:S(2)}, u32[]{:S(2)}) %collective-permute-start) | collective-permute-done | bytes 524320 | tf_op jit(solution)/shard_map/while/body/eval_jaxpr/ppermute | solution.py:13
  230.4 14.6 %collective-permute-done = bf16[2,128,1024]{1,2,0:T(8,128)(2,1)S(1)} collective-permute-done((bf16[2,128,1024]{1,2,0:T(8,128)(2,1)S(1)}, bf16[2,128,1024]{1,2,0:T(8,128)(2,1)S(1)}, u32[]{:S(2)}, u32[]{:S(2)}) %collective-permute-start) | collective-permute-done | bytes 524320 | tf_op jit(solution)/shard_map/while/body/eval_jaxpr/ppermute | solution.py:13
  249.0 15.8 %collective-permute-done = bf16[2,128,1024]{1,2,0:T(8,128)(2,1)S(1)} collective-permute-done((bf16[2,128,1024]{1,2,0:T(8,128)(2,1)S(1)}, bf16[2,128,1024]{1,2,0:T(8,128)(2,1)S(1)}, u32[]{:S(2)}, u32[]{:S(2)}) %collective-permute-start) | collective-permute-done | bytes 524320 | tf_op jit(solution)/shard_map/while/body/eval_jaxpr/ppermute | solution.py:13
  268.6 16.9 %collective-permute-done = bf16[2,128,1024]{1,2,0:T(8,128)(2,1)S(1)} collective-permute-done((bf16[2,128,1024]{1,2,0:T(8,128)(2,1)S(1)}, bf16[2,128,1024]{1,2,0:T(8,128)(2,1)S(1)}, u32[]{:S(2)}, u32[]{:S(2)}) %collective-permute-start) | collective-permute-done | bytes 524320 | tf_op jit(solution)/shard_map/while/body/eval_jaxpr/ppermute | solution.py:13
  289.4 16.8 %collective-permute-done = bf16[2,128,1024]{1,2,0:T(8,128)(2,1)S(1)} collective-permute-done((bf16[2,128,1024]{1,2,0:T(8,128)(2,1)S(1)}, bf16[2,128,1024]{1,2,0:T(8,128)(2,1)S(1)}, u32[]{:S(2)}, u32[]{:S(2)}) %collective-permute-start) | collective-permute-done | bytes 524320 | tf_op jit(solution)/shard_map/while/body/eval_jaxpr/ppermute | solution.py:13
  310.1 16.0 %collective-permute-done = bf16[2,128,1024]{1,2,0:T(8,128)(2,1)S(1)} collective-permute-done((bf16[2,128,1024]{1,2,0:T(8,128)(2,1)S(1)}, bf16[2,128,1024]{1,2,0:T(8,128)(2,1)S(1)}, u32[]{:S(2)}, u32[]{:S(2)}) %collective-permute-start) | collective-permute-done | bytes 524320 | tf_op jit(solution)/shard_map/while/body/eval_jaxpr/ppermute | solution.py:13
  330.0 15.1 %collective-permute-done = bf16[2,128,1024]{1,2,0:T(8,128)(2,1)S(1)} collective-permute-done((bf16[2,128,1024]{1,2,0:T(8,128)(2,1)S(1)}, bf16[2,128,1024]{1,2,0:T(8,128)(2,1)S(1)}, u32[]{:S(2)}, u32[]{:S(2)}) %collective-permute-start) | collective-permute-done | bytes 524320 | tf_op jit(solution)/shard_map/while/body/eval_jaxpr/ppermute | solution.py:13
  349.0 14.3 %collective-permute-done = bf16[2,128,1024]{1,2,0:T(8,128)(2,1)S(1)} collective-permute-done((bf16[2,128,1024]{1,2,0:T(8,128)(2,1)S(1)}, bf16[2,128,1024]{1,2,0:T(8,128)(2,1)S(1)}, u32[]{:S(2)}, u32[]{:S(2)}) %collective-permute-start) | collective-permute-done | bytes 524320 | tf_op jit(solution)/shard_map/while/body/eval_jaxpr/ppermute | solution.py:13
  367.1 13.4 %collective-permute-done = bf16[2,128,1024]{1,2,0:T(8,128)(2,1)S(1)} collective-permute-done((bf16[2,128,1024]{1,2,0:T(8,128)(2,1)S(1)}, bf16[2,128,1024]{1,2,0:T(8,128)(2,1)S(1)}, u32[]{:S(2)}, u32[]{:S(2)}) %collective-permute-start) | collective-permute-done | bytes 524320 | tf_op jit(solution)/shard_map/while/body/eval_jaxpr/ppermute | solution.py:13
  384.4 12.5 %collective-permute-done = bf16[2,128,1024]{1,2,0:T(8,128)(2,1)S(1)} collective-permute-done((bf16[2,128,1024]{1,2,0:T(8,128)(2,1)S(1)}, bf16[2,128,1024]{1,2,0:T(8,128)(2,1)S(1)}, u32[]{:S(2)}, u32[]{:S(2)}) %collective-permute-start) | collective-permute-done | bytes 524320 | tf_op jit(solution)/shard_map/while/body/eval_jaxpr/ppermute | solution.py:13
  400.9 11.8 %collective-permute-done = bf16[2,128,1024]{1,2,0:T(8,128)(2,1)S(1)} collective-permute-done((bf16[2,128,1024]{1,2,0:T(8,128)(2,1)S(1)}, bf16[2,128,1024]{1,2,0:T(8,128)(2,1)S(1)}, u32[]{:S(2)}, u32[]{:S(2)}) %collective-permute-start) | collective-permute-done | bytes 524320 | tf_op jit(solution)/shard_map/while/body/eval_jaxpr/ppermute | solution.py:13
  448.0 12.1 %collective-permute-done = bf16[2,128,1024]{1,2,0:T(8,128)(2,1)S(1)} collective-permute-done((bf16[2,128,1024]{1,2,0:T(8,128)(2,1)S(1)}, bf16[2,128,1024]{1,2,0:T(8,128)(2,1)S(1)}, u32[]{:S(2)}, u32[]{:S(2)}) %collective-permute-start) | collective-permute-done | bytes 524320 | tf_op jit(solution)/shard_map/while/body/eval_jaxpr/ppermute | solution.py:13
  464.0 13.2 %collective-permute-done = bf16[2,128,1024]{1,2,0:T(8,128)(2,1)S(1)} collective-permute-done((bf16[2,128,1024]{1,2,0:T(8,128)(2,1)S(1)}, bf16[2,128,1024]{1,2,0:T(8,128)(2,1)S(1)}, u32[]{:S(2)}, u32[]{:S(2)}) %collective-permute-start) | collective-permute-done | bytes 524320 | tf_op jit(solution)/shard_map/while/body/eval_jaxpr/ppermute | solution.py:13
  481.1 14.4 %collective-permute-done = bf16[2,128,1024]{1,2,0:T(8,128)(2,1)S(1)} collective-permute-done((bf16[2,128,1024]{1,2,0:T(8,128)(2,1)S(1)}, bf16[2,128,1024]{1,2,0:T(8,128)(2,1)S(1)}, u32[]{:S(2)}, u32[]{:S(2)}) %collective-permute-start) | collective-permute-done | bytes 524320 | tf_op jit(solution)/shard_map/while/body/eval_jaxpr/ppermute | solution.py:13
  499.4 15.5 %collective-permute-done = bf16[2,128,1024]{1,2,0:T(8,128)(2,1)S(1)} collective-permute-done((bf16[2,128,1024]{1,2,0:T(8,128)(2,1)S(1)}, bf16[2,128,1024]{1,2,0:T(8,128)(2,1)S(1)}, u32[]{:S(2)}, u32[]{:S(2)}) %collective-permute-start) | collective-permute-done | bytes 524320 | tf_op jit(solution)/shard_map/while/body/eval_jaxpr/ppermute | solution.py:13
  518.8 16.7 %collective-permute-done = bf16[2,128,1024]{1,2,0:T(8,128)(2,1)S(1)} collective-permute-done((bf16[2,128,1024]{1,2,0:T(8,128)(2,1)S(1)}, bf16[2,128,1024]{1,2,0:T(8,128)(2,1)S(1)}, u32[]{:S(2)}, u32[]{:S(2)}) %collective-permute-start) | collective-permute-done | bytes 524320 | tf_op jit(solution)/shard_map/while/body/eval_jaxpr/ppermute | solution.py:13
  539.4 17.0 %collective-permute-done = bf16[2,128,1024]{1,2,0:T(8,128)(2,1)S(1)} collective-permute-done((bf16[2,128,1024]{1,2,0:T(8,128)(2,1)S(1)}, bf16[2,128,1024]{1,2,0:T(8,128)(2,1)S(1)}, u32[]{:S(2)}, u32[]{:S(2)}) %collective-permute-start) | collective-permute-done | bytes 524320 | tf_op jit(solution)/shard_map/while/body/eval_jaxpr/ppermute | solution.py:13
  560.3 16.2 %collective-permute-done = bf16[2,128,1024]{1,2,0:T(8,128)(2,1)S(1)} collective-permute-done((bf16[2,128,1024]{1,2,0:T(8,128)(2,1)S(1)}, bf16[2,128,1024]{1,2,0:T(8,128)(2,1)S(1)}, u32[]{:S(2)}, u32[]{:S(2)}) %collective-permute-start) | collective-permute-done | bytes 524320 | tf_op jit(solution)/shard_map/while/body/eval_jaxpr/ppermute | solution.py:13
  580.4 14.4 %collective-permute-done = bf16[2,128,1024]{1,2,0:T(8,128)(2,1)S(1)} collective-permute-done((bf16[2,128,1024]{1,2,0:T(8,128)(2,1)S(1)}, bf16[2,128,1024]{1,2,0:T(8,128)(2,1)S(1)}, u32[]{:S(2)}, u32[]{:S(2)}) %collective-permute-start) | collective-permute-done | bytes 524320 | tf_op jit(solution)/shard_map/while/body/eval_jaxpr/ppermute | solution.py:13
  613.4 18.1 %all_to_all.10 = bf16[32,4,1,1024]{3,1,2,0:T(4,128)(2,1)S(1)} all-to-all(bf16[32,4,1,1024]{3,1,2,0:T(4,128)(2,1)S(1)} %constant_dynamic-update-slice_fusion), channel_id=1, replica_groups=mesh['dp'=16,'ctx'=32] {'ctx'}, dimensions={0} | all-to-all | bytes 524288 | tf_op jit(solution)/shard_map/all_to_all | solution.py:129
  (518 shorter events, 203.8 us)
Async XLA Ops:
  3.1 45.7 %collective-permute-start.1 = (bf16[127,1024]{0,1:T(8,128)(2,1)S(1)}, bf16[127,1024]{0,1:T(8,128)(2,1)S(1)}, u32[]{:S(2)}, u32[]{:S(2)}) collective-permute-start(bf16[127,1024]{0,1:T(8,128)(2,1)S(1)} %slice.26), channel_id=1, source_target_pairs={{0,1},{1,2},{2,3},{3,4},{4,5},{5,6},{6,7},{7,8},{8,9},{9,10},{10,1... | collective-permute-start | bytes 780296 | tf_op jit(solution)/shard_map/ppermute | solution.py:19
  8.4 47.8 %all-to-all-start = ((bf16[4,32,1024]{2,0,1:T(4,128)(2,1)}), bf16[4,32,1024]{2,0,1:T(4,128)(2,1)S(1)}, u32[]{:S(2)}, u32[]{:S(2)}) async-start(bf16[4,32,1024]{2,0,1:T(4,128)(2,1)} %copy.926), calls=%async_computation | async-start | bytes 524288 | tf_op jit(solution)/shard_map/all_to_all | solution.py:116
  57.6 18.3 %collective-permute-start = (bf16[2,128,1024]{1,2,0:T(8,128)(2,1)S(1)}, bf16[2,128,1024]{1,2,0:T(8,128)(2,1)S(1)}, u32[]{:S(2)}, u32[]{:S(2)}) collective-permute-start(bf16[2,128,1024]{1,2,0:T(8,128)(2,1)S(1)} %get-tuple-element.1022), channel_id=1, source_target_pairs={{0,1},{1,2},{2,3},{3,4},{4,5},{5,6},{6,7},{7,8},{8,9},{9,10},{10,1... | collective-permute-start | bytes 1572872 | tf_op jit(solution)/shard_map/while/body/eval_jaxpr/ppermute | solution.py:13
  77.2 17.5 %collective-permute-start = (bf16[2,128,1024]{1,2,0:T(8,128)(2,1)S(1)}, bf16[2,128,1024]{1,2,0:T(8,128)(2,1)S(1)}, u32[]{:S(2)}, u32[]{:S(2)}) collective-permute-start(bf16[2,128,1024]{1,2,0:T(8,128)(2,1)S(1)} %get-tuple-element.1022), channel_id=1, source_target_pairs={{0,1},{1,2},{2,3},{3,4},{4,5},{5,6},{6,7},{7,8},{8,9},{9,10},{10,1... | collective-permute-start | bytes 1572872 | tf_op jit(solution)/shard_map/while/body/eval_jaxpr/ppermute | solution.py:13
  96.0 16.6 %collective-permute-start = (bf16[2,128,1024]{1,2,0:T(8,128)(2,1)S(1)}, bf16[2,128,1024]{1,2,0:T(8,128)(2,1)S(1)}, u32[]{:S(2)}, u32[]{:S(2)}) collective-permute-start(bf16[2,128,1024]{1,2,0:T(8,128)(2,1)S(1)} %get-tuple-element.1022), channel_id=1, source_target_pairs={{0,1},{1,2},{2,3},{3,4},{4,5},{5,6},{6,7},{7,8},{8,9},{9,10},{10,1... | collective-permute-start | bytes 1572872 | tf_op jit(solution)/shard_map/while/body/eval_jaxpr/ppermute | solution.py:13
  113.9 15.7 %collective-permute-start = (bf16[2,128,1024]{1,2,0:T(8,128)(2,1)S(1)}, bf16[2,128,1024]{1,2,0:T(8,128)(2,1)S(1)}, u32[]{:S(2)}, u32[]{:S(2)}) collective-permute-start(bf16[2,128,1024]{1,2,0:T(8,128)(2,1)S(1)} %get-tuple-element.1022), channel_id=1, source_target_pairs={{0,1},{1,2},{2,3},{3,4},{4,5},{5,6},{6,7},{7,8},{8,9},{9,10},{10,1... | collective-permute-start | bytes 1572872 | tf_op jit(solution)/shard_map/while/body/eval_jaxpr/ppermute | solution.py:13
  131.0 14.9 %collective-permute-start = (bf16[2,128,1024]{1,2,0:T(8,128)(2,1)S(1)}, bf16[2,128,1024]{1,2,0:T(8,128)(2,1)S(1)}, u32[]{:S(2)}, u32[]{:S(2)}) collective-permute-start(bf16[2,128,1024]{1,2,0:T(8,128)(2,1)S(1)} %get-tuple-element.1022), channel_id=1, source_target_pairs={{0,1},{1,2},{2,3},{3,4},{4,5},{5,6},{6,7},{7,8},{8,9},{9,10},{10,1... | collective-permute-start | bytes 1572872 | tf_op jit(solution)/shard_map/while/body/eval_jaxpr/ppermute | solution.py:13
  147.2 14.4 %collective-permute-start = (bf16[2,128,1024]{1,2,0:T(8,128)(2,1)S(1)}, bf16[2,128,1024]{1,2,0:T(8,128)(2,1)S(1)}, u32[]{:S(2)}, u32[]{:S(2)}) collective-permute-start(bf16[2,128,1024]{1,2,0:T(8,128)(2,1)S(1)} %get-tuple-element.1022), channel_id=1, source_target_pairs={{0,1},{1,2},{2,3},{3,4},{4,5},{5,6},{6,7},{7,8},{8,9},{9,10},{10,1... | collective-permute-start | bytes 1572872 | tf_op jit(solution)/shard_map/while/body/eval_jaxpr/ppermute | solution.py:13
  162.9 14.4 %collective-permute-start = (bf16[2,128,1024]{1,2,0:T(8,128)(2,1)S(1)}, bf16[2,128,1024]{1,2,0:T(8,128)(2,1)S(1)}, u32[]{:S(2)}, u32[]{:S(2)}) collective-permute-start(bf16[2,128,1024]{1,2,0:T(8,128)(2,1)S(1)} %get-tuple-element.1022), channel_id=1, source_target_pairs={{0,1},{1,2},{2,3},{3,4},{4,5},{5,6},{6,7},{7,8},{8,9},{9,10},{10,1... | collective-permute-start | bytes 1572872 | tf_op jit(solution)/shard_map/while/body/eval_jaxpr/ppermute | solution.py:13
  178.6 14.4 %collective-permute-start = (bf16[2,128,1024]{1,2,0:T(8,128)(2,1)S(1)}, bf16[2,128,1024]{1,2,0:T(8,128)(2,1)S(1)}, u32[]{:S(2)}, u32[]{:S(2)}) collective-permute-start(bf16[2,128,1024]{1,2,0:T(8,128)(2,1)S(1)} %get-tuple-element.1022), channel_id=1, source_target_pairs={{0,1},{1,2},{2,3},{3,4},{4,5},{5,6},{6,7},{7,8},{8,9},{9,10},{10,1... | collective-permute-start | bytes 1572872 | tf_op jit(solution)/shard_map/while/body/eval_jaxpr/ppermute | solution.py:13
  194.3 14.9 %collective-permute-start = (bf16[2,128,1024]{1,2,0:T(8,128)(2,1)S(1)}, bf16[2,128,1024]{1,2,0:T(8,128)(2,1)S(1)}, u32[]{:S(2)}, u32[]{:S(2)}) collective-permute-start(bf16[2,128,1024]{1,2,0:T(8,128)(2,1)S(1)} %get-tuple-element.1022), channel_id=1, source_target_pairs={{0,1},{1,2},{2,3},{3,4},{4,5},{5,6},{6,7},{7,8},{8,9},{9,10},{10,1... | collective-permute-start | bytes 1572872 | tf_op jit(solution)/shard_map/while/body/eval_jaxpr/ppermute | solution.py:13
  210.5 16.0 %collective-permute-start = (bf16[2,128,1024]{1,2,0:T(8,128)(2,1)S(1)}, bf16[2,128,1024]{1,2,0:T(8,128)(2,1)S(1)}, u32[]{:S(2)}, u32[]{:S(2)}) collective-permute-start(bf16[2,128,1024]{1,2,0:T(8,128)(2,1)S(1)} %get-tuple-element.1022), channel_id=1, source_target_pairs={{0,1},{1,2},{2,3},{3,4},{4,5},{5,6},{6,7},{7,8},{8,9},{9,10},{10,1... | collective-permute-start | bytes 1572872 | tf_op jit(solution)/shard_map/while/body/eval_jaxpr/ppermute | solution.py:13
  227.9 17.2 %collective-permute-start = (bf16[2,128,1024]{1,2,0:T(8,128)(2,1)S(1)}, bf16[2,128,1024]{1,2,0:T(8,128)(2,1)S(1)}, u32[]{:S(2)}, u32[]{:S(2)}) collective-permute-start(bf16[2,128,1024]{1,2,0:T(8,128)(2,1)S(1)} %get-tuple-element.1022), channel_id=1, source_target_pairs={{0,1},{1,2},{2,3},{3,4},{4,5},{5,6},{6,7},{7,8},{8,9},{9,10},{10,1... | collective-permute-start | bytes 1572872 | tf_op jit(solution)/shard_map/while/body/eval_jaxpr/ppermute | solution.py:13
  246.4 18.3 %collective-permute-start = (bf16[2,128,1024]{1,2,0:T(8,128)(2,1)S(1)}, bf16[2,128,1024]{1,2,0:T(8,128)(2,1)S(1)}, u32[]{:S(2)}, u32[]{:S(2)}) collective-permute-start(bf16[2,128,1024]{1,2,0:T(8,128)(2,1)S(1)} %get-tuple-element.1022), channel_id=1, source_target_pairs={{0,1},{1,2},{2,3},{3,4},{4,5},{5,6},{6,7},{7,8},{8,9},{9,10},{10,1... | collective-permute-start | bytes 1572872 | tf_op jit(solution)/shard_map/while/body/eval_jaxpr/ppermute | solution.py:13
  266.0 19.5 %collective-permute-start = (bf16[2,128,1024]{1,2,0:T(8,128)(2,1)S(1)}, bf16[2,128,1024]{1,2,0:T(8,128)(2,1)S(1)}, u32[]{:S(2)}, u32[]{:S(2)}) collective-permute-start(bf16[2,128,1024]{1,2,0:T(8,128)(2,1)S(1)} %get-tuple-element.1022), channel_id=1, source_target_pairs={{0,1},{1,2},{2,3},{3,4},{4,5},{5,6},{6,7},{7,8},{8,9},{9,10},{10,1... | collective-permute-start | bytes 1572872 | tf_op jit(solution)/shard_map/while/body/eval_jaxpr/ppermute | solution.py:13
  286.8 19.4 %collective-permute-start = (bf16[2,128,1024]{1,2,0:T(8,128)(2,1)S(1)}, bf16[2,128,1024]{1,2,0:T(8,128)(2,1)S(1)}, u32[]{:S(2)}, u32[]{:S(2)}) collective-permute-start(bf16[2,128,1024]{1,2,0:T(8,128)(2,1)S(1)} %get-tuple-element.1022), channel_id=1, source_target_pairs={{0,1},{1,2},{2,3},{3,4},{4,5},{5,6},{6,7},{7,8},{8,9},{9,10},{10,1... | collective-permute-start | bytes 1572872 | tf_op jit(solution)/shard_map/while/body/eval_jaxpr/ppermute | solution.py:13
  307.5 18.5 %collective-permute-start = (bf16[2,128,1024]{1,2,0:T(8,128)(2,1)S(1)}, bf16[2,128,1024]{1,2,0:T(8,128)(2,1)S(1)}, u32[]{:S(2)}, u32[]{:S(2)}) collective-permute-start(bf16[2,128,1024]{1,2,0:T(8,128)(2,1)S(1)} %get-tuple-element.1022), channel_id=1, source_target_pairs={{0,1},{1,2},{2,3},{3,4},{4,5},{5,6},{6,7},{7,8},{8,9},{9,10},{10,1... | collective-permute-start | bytes 1572872 | tf_op jit(solution)/shard_map/while/body/eval_jaxpr/ppermute | solution.py:13
  327.4 17.7 %collective-permute-start = (bf16[2,128,1024]{1,2,0:T(8,128)(2,1)S(1)}, bf16[2,128,1024]{1,2,0:T(8,128)(2,1)S(1)}, u32[]{:S(2)}, u32[]{:S(2)}) collective-permute-start(bf16[2,128,1024]{1,2,0:T(8,128)(2,1)S(1)} %get-tuple-element.1022), channel_id=1, source_target_pairs={{0,1},{1,2},{2,3},{3,4},{4,5},{5,6},{6,7},{7,8},{8,9},{9,10},{10,1... | collective-permute-start | bytes 1572872 | tf_op jit(solution)/shard_map/while/body/eval_jaxpr/ppermute | solution.py:13
  346.4 16.8 %collective-permute-start = (bf16[2,128,1024]{1,2,0:T(8,128)(2,1)S(1)}, bf16[2,128,1024]{1,2,0:T(8,128)(2,1)S(1)}, u32[]{:S(2)}, u32[]{:S(2)}) collective-permute-start(bf16[2,128,1024]{1,2,0:T(8,128)(2,1)S(1)} %get-tuple-element.1022), channel_id=1, source_target_pairs={{0,1},{1,2},{2,3},{3,4},{4,5},{5,6},{6,7},{7,8},{8,9},{9,10},{10,1... | collective-permute-start | bytes 1572872 | tf_op jit(solution)/shard_map/while/body/eval_jaxpr/ppermute | solution.py:13
  364.5 16.0 %collective-permute-start = (bf16[2,128,1024]{1,2,0:T(8,128)(2,1)S(1)}, bf16[2,128,1024]{1,2,0:T(8,128)(2,1)S(1)}, u32[]{:S(2)}, u32[]{:S(2)}) collective-permute-start(bf16[2,128,1024]{1,2,0:T(8,128)(2,1)S(1)} %get-tuple-element.1022), channel_id=1, source_target_pairs={{0,1},{1,2},{2,3},{3,4},{4,5},{5,6},{6,7},{7,8},{8,9},{9,10},{10,1... | collective-permute-start | bytes 1572872 | tf_op jit(solution)/shard_map/while/body/eval_jaxpr/ppermute | solution.py:13
  381.8 15.1 %collective-permute-start = (bf16[2,128,1024]{1,2,0:T(8,128)(2,1)S(1)}, bf16[2,128,1024]{1,2,0:T(8,128)(2,1)S(1)}, u32[]{:S(2)}, u32[]{:S(2)}) collective-permute-start(bf16[2,128,1024]{1,2,0:T(8,128)(2,1)S(1)} %get-tuple-element.1022), channel_id=1, source_target_pairs={{0,1},{1,2},{2,3},{3,4},{4,5},{5,6},{6,7},{7,8},{8,9},{9,10},{10,1... | collective-permute-start | bytes 1572872 | tf_op jit(solution)/shard_map/while/body/eval_jaxpr/ppermute | solution.py:13
  398.3 14.4 %collective-permute-start = (bf16[2,128,1024]{1,2,0:T(8,128)(2,1)S(1)}, bf16[2,128,1024]{1,2,0:T(8,128)(2,1)S(1)}, u32[]{:S(2)}, u32[]{:S(2)}) collective-permute-start(bf16[2,128,1024]{1,2,0:T(8,128)(2,1)S(1)} %get-tuple-element.1022), channel_id=1, source_target_pairs={{0,1},{1,2},{2,3},{3,4},{4,5},{5,6},{6,7},{7,8},{8,9},{9,10},{10,1... | collective-permute-start | bytes 1572872 | tf_op jit(solution)/shard_map/while/body/eval_jaxpr/ppermute | solution.py:13
  429.7 14.4 %collective-permute-start = (bf16[2,128,1024]{1,2,0:T(8,128)(2,1)S(1)}, bf16[2,128,1024]{1,2,0:T(8,128)(2,1)S(1)}, u32[]{:S(2)}, u32[]{:S(2)}) collective-permute-start(bf16[2,128,1024]{1,2,0:T(8,128)(2,1)S(1)} %get-tuple-element.1022), channel_id=1, source_target_pairs={{0,1},{1,2},{2,3},{3,4},{4,5},{5,6},{6,7},{7,8},{8,9},{9,10},{10,1... | collective-permute-start | bytes 1572872 | tf_op jit(solution)/shard_map/while/body/eval_jaxpr/ppermute | solution.py:13
  445.4 14.7 %collective-permute-start = (bf16[2,128,1024]{1,2,0:T(8,128)(2,1)S(1)}, bf16[2,128,1024]{1,2,0:T(8,128)(2,1)S(1)}, u32[]{:S(2)}, u32[]{:S(2)}) collective-permute-start(bf16[2,128,1024]{1,2,0:T(8,128)(2,1)S(1)} %get-tuple-element.1022), channel_id=1, source_target_pairs={{0,1},{1,2},{2,3},{3,4},{4,5},{5,6},{6,7},{7,8},{8,9},{9,10},{10,1... | collective-permute-start | bytes 1572872 | tf_op jit(solution)/shard_map/while/body/eval_jaxpr/ppermute | solution.py:13
  461.4 15.8 %collective-permute-start = (bf16[2,128,1024]{1,2,0:T(8,128)(2,1)S(1)}, bf16[2,128,1024]{1,2,0:T(8,128)(2,1)S(1)}, u32[]{:S(2)}, u32[]{:S(2)}) collective-permute-start(bf16[2,128,1024]{1,2,0:T(8,128)(2,1)S(1)} %get-tuple-element.1022), channel_id=1, source_target_pairs={{0,1},{1,2},{2,3},{3,4},{4,5},{5,6},{6,7},{7,8},{8,9},{9,10},{10,1... | collective-permute-start | bytes 1572872 | tf_op jit(solution)/shard_map/while/body/eval_jaxpr/ppermute | solution.py:13
  478.5 17.0 %collective-permute-start = (bf16[2,128,1024]{1,2,0:T(8,128)(2,1)S(1)}, bf16[2,128,1024]{1,2,0:T(8,128)(2,1)S(1)}, u32[]{:S(2)}, u32[]{:S(2)}) collective-permute-start(bf16[2,128,1024]{1,2,0:T(8,128)(2,1)S(1)} %get-tuple-element.1022), channel_id=1, source_target_pairs={{0,1},{1,2},{2,3},{3,4},{4,5},{5,6},{6,7},{7,8},{8,9},{9,10},{10,1... | collective-permute-start | bytes 1572872 | tf_op jit(solution)/shard_map/while/body/eval_jaxpr/ppermute | solution.py:13
  496.8 18.1 %collective-permute-start = (bf16[2,128,1024]{1,2,0:T(8,128)(2,1)S(1)}, bf16[2,128,1024]{1,2,0:T(8,128)(2,1)S(1)}, u32[]{:S(2)}, u32[]{:S(2)}) collective-permute-start(bf16[2,128,1024]{1,2,0:T(8,128)(2,1)S(1)} %get-tuple-element.1022), channel_id=1, source_target_pairs={{0,1},{1,2},{2,3},{3,4},{4,5},{5,6},{6,7},{7,8},{8,9},{9,10},{10,1... | collective-permute-start | bytes 1572872 | tf_op jit(solution)/shard_map/while/body/eval_jaxpr/ppermute | solution.py:13
  516.2 19.3 %collective-permute-start = (bf16[2,128,1024]{1,2,0:T(8,128)(2,1)S(1)}, bf16[2,128,1024]{1,2,0:T(8,128)(2,1)S(1)}, u32[]{:S(2)}, u32[]{:S(2)}) collective-permute-start(bf16[2,128,1024]{1,2,0:T(8,128)(2,1)S(1)} %get-tuple-element.1022), channel_id=1, source_target_pairs={{0,1},{1,2},{2,3},{3,4},{4,5},{5,6},{6,7},{7,8},{8,9},{9,10},{10,1... | collective-permute-start | bytes 1572872 | tf_op jit(solution)/shard_map/while/body/eval_jaxpr/ppermute | solution.py:13
  536.8 19.6 %collective-permute-start = (bf16[2,128,1024]{1,2,0:T(8,128)(2,1)S(1)}, bf16[2,128,1024]{1,2,0:T(8,128)(2,1)S(1)}, u32[]{:S(2)}, u32[]{:S(2)}) collective-permute-start(bf16[2,128,1024]{1,2,0:T(8,128)(2,1)S(1)} %get-tuple-element.1022), channel_id=1, source_target_pairs={{0,1},{1,2},{2,3},{3,4},{4,5},{5,6},{6,7},{7,8},{8,9},{9,10},{10,1... | collective-permute-start | bytes 1572872 | tf_op jit(solution)/shard_map/while/body/eval_jaxpr/ppermute | solution.py:13
  557.8 18.8 %collective-permute-start = (bf16[2,128,1024]{1,2,0:T(8,128)(2,1)S(1)}, bf16[2,128,1024]{1,2,0:T(8,128)(2,1)S(1)}, u32[]{:S(2)}, u32[]{:S(2)}) collective-permute-start(bf16[2,128,1024]{1,2,0:T(8,128)(2,1)S(1)} %get-tuple-element.1022), channel_id=1, source_target_pairs={{0,1},{1,2},{2,3},{3,4},{4,5},{5,6},{6,7},{7,8},{8,9},{9,10},{10,1... | collective-permute-start | bytes 1572872 | tf_op jit(solution)/shard_map/while/body/eval_jaxpr/ppermute | solution.py:13
  577.8 16.9 %collective-permute-start = (bf16[2,128,1024]{1,2,0:T(8,128)(2,1)S(1)}, bf16[2,128,1024]{1,2,0:T(8,128)(2,1)S(1)}, u32[]{:S(2)}, u32[]{:S(2)}) collective-permute-start(bf16[2,128,1024]{1,2,0:T(8,128)(2,1)S(1)} %get-tuple-element.1022), channel_id=1, source_target_pairs={{0,1},{1,2},{2,3},{3,4},{4,5},{5,6},{6,7},{7,8},{8,9},{9,10},{10,1... | collective-permute-start | bytes 1572872 | tf_op jit(solution)/shard_map/while/body/eval_jaxpr/ppermute | solution.py:13
  596.1 14.4 %collective-permute-start = (bf16[2,128,1024]{1,2,0:T(8,128)(2,1)S(1)}, bf16[2,128,1024]{1,2,0:T(8,128)(2,1)S(1)}, u32[]{:S(2)}, u32[]{:S(2)}) collective-permute-start(bf16[2,128,1024]{1,2,0:T(8,128)(2,1)S(1)} %get-tuple-element.1022), channel_id=1, source_target_pairs={{0,1},{1,2},{2,3},{3,4},{4,5},{5,6},{6,7},{7,8},{8,9},{9,10},{10,1... | collective-permute-start | bytes 1572872 | tf_op jit(solution)/shard_map/while/body/eval_jaxpr/ppermute | solution.py:13
  (5 other events, 48.8 us)
